TPU v7x, 32 devices: a whole 2x2x4 slice. The times are simulated.
32 devices in a mesh: groups: 2 (over y), picks: 4 (over z), heads: 4 (over x, core).
Axes of the slice: x: 2, y: 2, z: 4, core: 2. Of those that a mesh axis runs over, the one named last changes fastest.
Arguments:
- coords: float32 [3, 8192], P(None, ('groups', 'picks')), parts along dimension 1, may hold values from -1 to 1
- horizon_ids: int32 [8192], P(('groups', 'picks')), parts along dimension 0, may hold values from 0 to 63
- horizon_levels: float32 [128], P('groups'), parts along dimension 0, may hold values from -2 to 2
- latents: bfloat16 [512, 1024], replicated, may hold values from -960 to 960
- kv_weight: bfloat16 [3072, 2, 1024], P('picks', None, 'heads'), may hold values from -0.109375 to 0.109375
- cross_out: bfloat16 [1024, 1024], P('heads'), may hold values from -0.75 to 0.75
- norm_gains: float32 [2, 1024], replicated, may hold values from 0.1 to 1.9
- self_qkv: bfloat16 [3, 1024, 1024], P(None, None, 'heads'), may hold values from -0.1875 to 0.1875
- self_out: bfloat16 [1024, 1024], P(None, 'heads'), may hold values from -0.1875 to 0.1875
- dec_kv: bfloat16 [2, 1024, 1024], P(None, None, 'heads'), may hold values from -0.1875 to 0.1875
- dec_query: bfloat16 [3072, 1024], P('picks', 'heads'), may hold values from -0.109375 to 0.109375
- readout: float32 [1024], P('heads'), may hold values from -0.1875 to 0.1875
Outputs:
- field: float32 [8192], P(('groups', 'picks')), parts along dimension 0
- latents_out: float32 [1024, 1024], P('groups', 'heads'), parts along dimension 0
- grad_query: float32 [6144, 1024], P(('groups', 'picks'), 'heads'), parts along dimension 0
There are 2 independent parts, one for each index of `groups`. A program takes and returns all parts, laid end to end along the dimension named above; an argument that names none is the same for every part. Nothing has to cross between parts.
All inputs are finite; a program needn't handle non-finite values.
Results may differ from a plain program's by a relative error of at most 0.028.
Values may be sent and summed in bfloat16 or wider, within the bound.
No kernel may reach another device: no remote copies, remote signals or barrier semaphores. Data moves between devices by JAX's collectives and lax.ppermute only.
A program may use at most 64 MiB of HBM per device.

v0:
```python
import functools
import jax
import jax.numpy as jnp
from jax import lax
from jax.sharding import PartitionSpec as P

HEAD = 128
BANDS = 512
HORIZONS = 64
PI = 3.141592653589793
EPS = 1e-06
RING_MAX = 4


def encode(coords):
    freq = jnp.linspace(1.0, BANDS / 2.0, BANDS).astype(jnp.float32)
    angle = PI * freq[None, :, None] * coords[:, None, :]
    table = jnp.concatenate([jnp.sin(angle), jnp.cos(angle)], axis=0)
    return table.reshape(6 * BANDS, coords.shape[1]).T.astype(jnp.bfloat16)


def ring_gather(x, axis, n):
    if n == 1:
        return x
    if n > RING_MAX:
        return lax.all_gather(x, axis, axis=0, tiled=True)
    idx = lax.axis_index(axis)
    blocks = [x]
    for s in range(1, n):
        blocks.append(lax.ppermute(x, axis, [(i, (i - s) % n) for i in range(n)]))
    flipped = jnp.stack(blocks)
    ordered = jnp.roll(flipped, idx, axis=0)
    return ordered.reshape((n * x.shape[0],) + x.shape[1:])


def fetch_rows(kv_weight, n_picks, n_groups):
    if n_groups != 2:
        return lax.all_gather(kv_weight, "picks", axis=0, tiled=True)
    g = lax.axis_index("groups")
    rows = kv_weight.shape[0] // 2
    mine = lax.dynamic_slice_in_dim(kv_weight, g * rows, rows, 0)
    first = max(8, 2 * rows // 3 // 8 * 8)
    bounds = [(0, first), (first, rows)] if first < rows else [(0, rows)]
    own, other = ([], [])
    for lo, hi in bounds:
        gathered = lax.all_gather(mine[lo:hi], "picks", axis=0, tiled=False)
        own.append(gathered)
        other.append(lax.ppermute(gathered, "groups", [(0, 1), (1, 0)]))
    halves = jnp.stack([jnp.concatenate(own, axis=1), jnp.concatenate(other, axis=1)], axis=1)
    halves = jnp.roll(halves, g, axis=1)
    return halves.reshape((n_picks * kv_weight.shape[0],) + kv_weight.shape[1:])


def pair_sum(x, axis, n):
    if n != 4:
        return lax.psum(x, axis)
    x = x + lax.ppermute(x, axis, [(k, k ^ 1) for k in range(n)])
    return x + lax.ppermute(x, axis, [(k, k ^ 2) for k in range(n)])


def on_device(
    coords,
    horizon_ids,
    horizon_levels,
    latents,
    kv_weight,
    cross_out,
    norm_gains,
    self_qkv,
    self_out,
    dec_kv,
    dec_query,
    readout,
    *,
    n_picks,
    n_heads,
    n_groups
):
    high = lax.Precision.HIGHEST
    scale = HEAD ** (-0.5)
    count = coords.shape[1]
    width = latents.shape[1]
    lat_rows = latents.shape[0]
    local = kv_weight.shape[2]
    nheads = local // HEAD
    column = lax.axis_index("heads") * local
    enc = encode(coords)
    cross_full = ring_gather(cross_out, "heads", n_heads)
    piece = lax.all_gather(kv_weight, "picks", axis=0, tiled=True)
    cross_full, piece = lax.optimization_barrier((cross_full, piece))
    keys_vals = jnp.einsum("tf,fjc->tjc", enc, piece, preferred_element_type=jnp.float32).astype(
        jnp.bfloat16
    )
    keys = keys_vals[:, 0].reshape(count, nheads, HEAD)
    values = keys_vals[:, 1].reshape(count, nheads, HEAD)
    queries = lax.dynamic_slice_in_dim(latents, column, local, 1).reshape(lat_rows, nheads, HEAD)
    scores = jnp.einsum("lhc,thc->hlt", queries, keys, preferred_element_type=jnp.float32) * scale
    top = jnp.max(scores, axis=2)
    expo = jnp.exp(scores - top[:, :, None])
    total = jnp.sum(expo, axis=2)
    numer = jnp.einsum(
        "hlt,thc->hlc", expo.astype(jnp.bfloat16), values, preferred_element_type=jnp.float32
    )
    all_numer = lax.all_gather(numer.astype(jnp.bfloat16), "picks", axis=0, tiled=False)
    all_stats = lax.all_gather(jnp.stack([top, total]), "picks", axis=0, tiled=False)
    best = jnp.max(all_stats[:, 0], axis=0)
    factor = jnp.exp(all_stats[:, 0] - best[None])
    merged_total = jnp.sum(factor * all_stats[:, 1], axis=0)
    merged_numer = jnp.einsum(
        "phl,phlc->hlc", factor, all_numer.astype(jnp.float32), precision=high
    )
    attended = (
        (merged_numer / merged_total[:, :, None])
        .transpose(1, 0, 2)
        .reshape(lat_rows, local)
        .astype(jnp.bfloat16)
    )
    out_full = ring_gather(self_out.T, "heads", n_heads).T
    out_full, attended = lax.optimization_barrier((out_full, attended))
    dq_local, attended = lax.optimization_barrier((dec_query, attended))
    dq_full = lax.all_gather(dq_local, "picks", axis=0, tiled=True)
    attended_full = ring_gather(attended.T, "heads", n_heads).T
    whole = latents.astype(jnp.float32) + jnp.dot(
        attended_full, cross_full, preferred_element_type=jnp.float32
    )
    power = jnp.mean(whole * whole, axis=1, keepdims=True)
    normed = (whole * lax.rsqrt(power + EPS) * norm_gains[0][None, :]).astype(jnp.bfloat16)
    state = lax.dynamic_slice_in_dim(whole, column, local, 1)
    qkv = jnp.einsum("ld,kde->kle", normed, self_qkv, preferred_element_type=jnp.float32).astype(
        jnp.bfloat16
    )
    self_q = qkv[0].reshape(lat_rows, nheads, HEAD)
    self_k = qkv[1].reshape(lat_rows, nheads, HEAD)
    self_v = qkv[2].reshape(lat_rows, nheads, HEAD)
    inner = jnp.einsum("lhc,mhc->hlm", self_q, self_k, preferred_element_type=jnp.float32) * scale
    raised = jnp.exp(inner)
    probs = (raised / jnp.sum(raised, axis=2, keepdims=True)).astype(jnp.bfloat16)
    head_out = (
        jnp.einsum("hlm,mhc->lhc", probs, self_v, preferred_element_type=jnp.float32)
        .astype(jnp.bfloat16)
        .reshape(lat_rows, local)
    )
    every_head = ring_gather(head_out.T, "heads", n_heads).T
    out_whole = whole + jnp.dot(every_head, out_full, preferred_element_type=jnp.float32)
    latents_out = lax.dynamic_slice_in_dim(out_whole, column, local, 1)
    power_two = jnp.mean(out_whole * out_whole, axis=1, keepdims=True)
    normed2 = (out_whole * lax.rsqrt(power_two + EPS) * norm_gains[1][None, :]).astype(jnp.bfloat16)
    dec = jnp.einsum("ld,kde->kle", normed2, dec_kv, preferred_element_type=jnp.float32).astype(
        jnp.bfloat16
    )
    dec_keys = dec[0].reshape(lat_rows, nheads, HEAD)
    dec_vals = dec[1].reshape(lat_rows, nheads, HEAD)
    query = jnp.dot(enc, dq_full, preferred_element_type=jnp.float32).astype(jnp.bfloat16)
    dec_q = query.reshape(count, nheads, HEAD)
    logits = jnp.einsum("thc,lhc->htl", dec_q, dec_keys, preferred_element_type=jnp.float32) * scale
    lifted = jnp.exp(logits)
    weights = lifted / jnp.sum(lifted, axis=2, keepdims=True)
    out = jnp.einsum(
        "htl,lhc->thc", weights.astype(jnp.bfloat16), dec_vals, preferred_element_type=jnp.float32
    )
    read = readout.reshape(nheads, HEAD)
    onehot = (horizon_ids[:, None] == jnp.arange(HORIZONS, dtype=jnp.int32)[None, :]).astype(
        jnp.float32
    )
    target = jnp.sum(onehot * horizon_levels[None, :], axis=1)
    value_read = jnp.einsum("lhc,hc->hl", dec_vals.astype(jnp.float32), read, precision=high)
    lever = (
        weights
        * (
            value_read[:, None, :]
            - jnp.sum(value_read[:, None, :] * weights, axis=2, keepdims=True)
        )
    ).astype(jnp.bfloat16)
    pull = jnp.einsum("htl,lhc->thc", lever, dec_keys, preferred_element_type=jnp.float32) * scale
    field = pair_sum(jnp.sum(out * read[None, :, :], axis=(1, 2)), "heads", n_heads)
    miss = field - target
    dquery = (miss[:, None, None] * pull).reshape(count, local).astype(jnp.bfloat16)
    grad_query = lax.psum_scatter(
        jnp.dot(enc.T, dquery, preferred_element_type=jnp.float32).astype(jnp.bfloat16),
        "picks",
        scatter_dimension=0,
        tiled=True,
    ).astype(jnp.float32)
    return (field, latents_out, grad_query)


def solution(mesh):
    in_specs = (
        P(None, ("groups", "picks")),
        P(("groups", "picks")),
        P("groups"),
        P(),
        P("picks", None, "heads"),
        P("heads", None),
        P(),
        P(None, None, "heads"),
        P(None, "heads"),
        P(None, None, "heads"),
        P("picks", "heads"),
        P("heads"),
    )
    out_specs = (P(("groups", "picks")), P("groups", "heads"), P(("groups", "picks"), "heads"))
    body = functools.partial(
        on_device,
        n_picks=mesh.shape["picks"],
        n_heads=mesh.shape["heads"],
        n_groups=mesh.shape["groups"],
    )
    return jax.shard_map(body, mesh=mesh, in_specs=in_specs, out_specs=out_specs, check_vma=False)
```

profile of v0, /device:TPU:0, one launch (start us, length us, event | category | flops | bytes accessed | tf_op | source)
XLA Modules:
  0.0 216.1 jit_solution(17237952158772773728)
XLA Ops:
  8.0 1.2 copy.60
  9.2 2.4 %collective-permute-start = (bf16[256,1024]{1,0:T(8,128)(2,1)S(1)}, bf16[256,1024]{1,0:T(8,128)(2,1)S(1)}, u32[]{:S(2)}, u32[]{:S(2)}) collective-permute-start(bf16[256,1024]{1,0:T(8,128)(2,1)S(1)} %bitcast.124), channel_id=1, source_target_pairs={{0,3},{1,0},{2,1},{3,2},{4,7},{5,4},{6,5},{7,6},{8,11},{9,8},{10,9... | collective-permute-start | bytes 1572872 | tf_op jit(solution)/shard_map/ppermute | solution.py:30
  12.4 1.7 collective-permute-start.4
  15.3 22.8 %fusion = (bf16[3,512,1024]{2,1,0:T(8,128)(2,1)S(1)}, bf16[3,512,1024]{2,1,0:T(8,128)(2,1)S(1)}) fusion(f32[3,1024]{1,0:T(4,128)S(1)} %copy-done.9, f32[512]{0:T(512)S(1)} %maximum_multiply_fusion), kind=kLoop, calls=%fused_computation.2 | loop fusion | flops 4718592 | bytes 6305792 | tf_op jit(solution)/shard_map/convert
  38.2 3.2 %pad_maximum_fusion = bf16[6,512,1024]{2,1,0:T(8,128)(2,1)} fusion(bf16[3,512,1024]{2,1,0:T(8,128)(2,1)S(1)} %get-tuple-element.29, bf16[3,512,1024]{2,1,0:T(8,128)(2,1)S(1)} %get-tuple-element.28), kind=kLoop, calls=%fused_computation.4 | loop fusion | flops 3145728 | bytes 12582912 | tf_op jit(solution)/shard_map/concatenate | solution.py:18
  41.4 5.1 %collective-permute-done.3 = bf16[256,1024]{1,0:T(8,128)(2,1)} collective-permute-done((bf16[256,1024]{1,0:T(8,128)(2,1)}, bf16[256,1024]{1,0:T(8,128)(2,1)}, u32[]{:S(2)}, u32[]{:S(2)}) %collective-permute-start.3) | collective-permute-done | bytes 524320 | tf_op jit(solution)/shard_map/ppermute | solution.py:30
  47.5 8.8 %collective-permute-done.4 = bf16[256,1024]{1,0:T(8,128)(2,1)} collective-permute-done((bf16[256,1024]{1,0:T(8,128)(2,1)}, bf16[256,1024]{1,0:T(8,128)(2,1)}, u32[]{:S(2)}, u32[]{:S(2)}) %collective-permute-start.4) | collective-permute-done | bytes 524320 | tf_op jit(solution)/shard_map/ppermute | solution.py:30
  56.3 5.1 %fusion.14 = bf16[4,256,1024]{2,1,0:T(8,128)(2,1)} fusion(s32[]{:T(128)S(6)} %select_n.27, bf16[1,256,1024]{2,1,0:T(8,128)(2,1)S(1)} %bitcast.143, bf16[1,256,1024]{2,1,0:T(8,128)(2,1)} %bitcast.13, bf16[1,256,1024]{2,1,0:T(8,128)(2,1)} %bitcast.14, bf16[1,256,1024]{2,1,0:T(8,128)(2,1)} %bitcast.15), kind=kLoop, calls=%fused_computation.38 | loop fusion | flops 7340032 | bytes 4194308 | tf_op jit(solution)/shard_map/jit(_roll_dynamic)/concatenate | solution.py:32
  61.4 14.5 %all-gather.6.cloned.1.call-done = bf16[3072,2,256]{2,1,0:T(2,128)(2,1)} async-done(((bf16[768,2,256]{2,1,0:T(2,128)(2,1)}), bf16[3072,2,256]{2,1,0:T(2,128)(2,1)}) %all-gather.6.cloned.1.call-update) | async-done | bytes 3145744 | tf_op jit(solution)/shard_map/all_gather | solution.py:89
  75.8 7.1 %fusion.32 = bf16[1024,2,256]{0,2,1:T(8,128)(2,1)S(1)} fusion(bf16[3072,1024,1]{1,0,2:T(8,128)(2,1)} %bitcast.118, bf16[3072,2,256]{2,1,0:T(2,128)(2,1)} %all-gather.6.cloned.1.call-done), kind=kOutput, calls=%fused_computation.81 | convolution fusion | flops 3221749760 | bytes 10485760 | tf_op jit(solution)/shard_map/tf,fjc->tjc/dot_general | solution.py:91
  83.9 2.0 copy-done.1
  86.0 1.6 fusion.43
  87.9 4.8 %fusion.21 = bf16[4,256,1024]{2,1,0:T(8,128)(2,1)} fusion(s32[]{:T(128)S(6)} %select_n.27, bf16[1,256,1024]{2,1,0:T(8,128)(2,1)S(1)} %bitcast.127, bf16[1,256,1024]{2,1,0:T(8,128)(2,1)S(1)} %bitcast.144, bf16[1,256,1024]{2,1,0:T(8,128)(2,1)} %bitcast.5, bf16[1,256,1024]{2,1,0:T(8,128)(2,1)} %bitcast.6), kind=kLoop, calls=%fused_computation.45 | loop fusion | flops 7340032 | bytes 4194308 | tf_op jit(solution)/shard_map/jit(_roll_dynamic)/concatenate | solution.py:32
  93.6 13.3 %all-gather.1 = f32[8,2,512]{2,1,0:T(2,128)S(1)} all-gather(f32[2,2,512]{2,1,0:T(2,128)S(1)} %pad_maximum_fusion.1), channel_id=3, replica_groups=mesh['groups'=2,'picks'=4,'heads'=4] {'picks'}, dimensions={0}, use_global_device_ids=true | all-gather | bytes 40960 | tf_op jit(solution)/shard_map/all_gather | solution.py:105
  106.9 7.8 %all-gather.10.cloned.1.call-done = bf16[8,512,128]{2,1,0:T(8,128)(2,1)} async-done(((bf16[2,512,128]{2,1,0:T(8,128)(2,1)}), bf16[8,512,128]{2,1,0:T(8,128)(2,1)}) %all-gather.10.cloned.1.call-update) | async-done | bytes 1048592 | tf_op jit(solution)/shard_map/all_gather | solution.py:104
  114.7 1.8 multiply_reduce_fusion.2
  118.6 5.6 %collective-permute-done.6 = bf16[256,512]{1,0:T(8,128)(2,1)S(1)} collective-permute-done((bf16[256,512]{1,0:T(8,128)(2,1)S(1)}, bf16[256,512]{1,0:T(8,128)(2,1)S(1)}, u32[]{:S(2)}, u32[]{:S(2)}) %collective-permute-start.6) | collective-permute-done | bytes 262176 | tf_op jit(solution)/shard_map/ppermute | solution.py:30
  124.2 6.7 %collective-permute-done.7 = bf16[256,512]{1,0:T(8,128)(2,1)S(1)} collective-permute-done((bf16[256,512]{1,0:T(8,128)(2,1)S(1)}, bf16[256,512]{1,0:T(8,128)(2,1)S(1)}, u32[]{:S(2)}, u32[]{:S(2)}) %collective-permute-start.7) | collective-permute-done | bytes 262176 | tf_op jit(solution)/shard_map/ppermute | solution.py:30
  131.1 2.2 %fusion.60 = bf16[4,256,512]{2,1,0:T(8,128)(2,1)S(1)} fusion(s32[]{:T(128)S(6)} %select_n.27, bf16[1,256,512]{2,1,0:T(8,128)(2,1)S(1)} %bitcast.133, bf16[1,256,512]{2,1,0:T(8,128)(2,1)S(1)} %bitcast.147, bf16[1,256,512]{2,1,0:T(8,128)(2,1)S(1)} %bitcast.148, bf16[1,256,512]{2,1,0:T(8,128)(2,1)} %bitcast.32), kind=kLoop, calls=%fused_computation.103 | loop fusion | flops 3670016 | bytes 2097156 | tf_op jit(solution)/shard_map/jit(_roll_dynamic)/concatenate | solution.py:32
  133.4 1.4 multiply_reduce_fusion.4
  137.1 1.5 collective-permute-start.10
  138.9 4.0 %collective-permute-done.9 = bf16[256,512]{1,0:T(8,128)(2,1)S(1)} collective-permute-done((bf16[256,512]{1,0:T(8,128)(2,1)S(1)}, bf16[256,512]{1,0:T(8,128)(2,1)S(1)}, u32[]{:S(2)}, u32[]{:S(2)}) %collective-permute-start.9) | collective-permute-done | bytes 262176 | tf_op jit(solution)/shard_map/ppermute | solution.py:30
  142.9 8.3 %collective-permute-done.10 = bf16[256,512]{1,0:T(8,128)(2,1)S(1)} collective-permute-done((bf16[256,512]{1,0:T(8,128)(2,1)S(1)}, bf16[256,512]{1,0:T(8,128)(2,1)S(1)}, u32[]{:S(2)}, u32[]{:S(2)}) %collective-permute-start.10) | collective-permute-done | bytes 262176 | tf_op jit(solution)/shard_map/ppermute | solution.py:30
  152.6 1.4 multiply_reduce_fusion.3
  154.0 1.3 copy-done.4
  156.3 5.1 %convolution_convert_fusion.2 = bf16[1024,256]{0,1:T(8,128)(2,1)S(1)} fusion(bf16[3072,1024]{1,0:T(8,128)(2,1)} %bitcast.119, bf16[3072,256]{1,0:T(8,128)(2,1)} %all-gather.8.cloned.1.call-done), kind=kOutput, calls=%fused_computation.84 | convolution fusion | flops 1610874880 | bytes 8388608 | tf_op jit(solution)/shard_map/dot_general | solution.py:153
  166.1 1.9 collective-permute-done.13
  168.6 1.2 multiply_convert_fusion.4
  170.2 3.1 %convolution_convert_fusion = bf16[3072,256]{1,0:T(8,128)(2,1)} fusion(bf16[3072,1024]{1,0:T(8,128)(2,1)S(1)} %bitcast.122, bf16[1024,256]{0,1:T(8,128)(2,1)S(1)} %bitcast.168), kind=kOutput, calls=%fused_computation.26 | convolution fusion | flops 1611399168 | bytes 8388608 | tf_op jit(solution)/shard_map/dot_general | solution.py:179
  173.4 1.9 constant_dynamic-slice_fusion
  175.2 32.4 %reduce-scatter.2.cloned.1.call-done = bf16[768,256]{1,0:T(8,128)(2,1)} async-done(((bf16[3072,256]{1,0:T(8,128)(2,1)}), bf16[768,256]{1,0:T(8,128)(2,1)}) %reduce-scatter.2.cloned.1.call-update) | async-done | bytes 393232 | tf_op jit(solution)/shard_map/reduce_scatter | solution.py:178
  207.6 1.9 convert_element_type.100
  (88 shorter events, 18.9 us)
Async XLA Ops:
  7.2 127.6 %copy-start = (bf16[3,1024,256]{2,1,0:T(8,128)(2,1)S(1)}, bf16[3,1024,256]{2,1,0:T(8,128)(2,1)}, u32[]{:S(2)}) copy-start(bf16[3,1024,256]{2,1,0:T(8,128)(2,1)} %param.23) | copy-start | bytes 4718596
  7.2 8.1 %copy-start.9 = (f32[3,1024]{1,0:T(4,128)S(1)}, f32[3,1024]{1,0:T(4,128)}, u32[]{:S(2)}) copy-start(f32[3,1024]{1,0:T(4,128)} %param.16) | copy-start | bytes 36868
  7.2 68.7 %all-gather.6.cloned.1.call-start = ((), (), s32[]{:S(2)}) async-start(), calls=%async_computation.1 | async-start | bytes 3932160 | tf_op jit(solution)/shard_map/all_gather | solution.py:89
  7.9 106.8 %all-gather.10.cloned.1.call-start = ((), (), s32[]{:S(2)}) async-start(), calls=%async_computation.4 | async-start | bytes 1310720 | tf_op jit(solution)/shard_map/all_gather | solution.py:104
  9.2 78.6 %collective-permute-start = (bf16[256,1024]{1,0:T(8,128)(2,1)S(1)}, bf16[256,1024]{1,0:T(8,128)(2,1)S(1)}, u32[]{:S(2)}, u32[]{:S(2)}) collective-permute-start(bf16[256,1024]{1,0:T(8,128)(2,1)S(1)} %bitcast.124), channel_id=1, source_target_pairs={{0,3},{1,0},{2,1},{3,2},{4,7},{5,4},{6,5},{7,6},{8,11},{9,8},{10,9... | collective-permute-start | bytes 1572872 | tf_op jit(solution)/shard_map/ppermute | solution.py:30
  11.7 76.2 %collective-permute-start.1 = (bf16[256,1024]{1,0:T(8,128)(2,1)S(1)}, bf16[256,1024]{1,0:T(8,128)(2,1)}, u32[]{:S(2)}, u32[]{:S(2)}) collective-permute-start(bf16[256,1024]{1,0:T(8,128)(2,1)S(1)} %bitcast.125), channel_id=1, source_target_pairs={{0,2},{1,3},{2,0},{3,1},{4,6},{5,7},{6,4},{7,5},{8,10},{9,11},{10,... | collective-permute-start | bytes 1572872 | tf_op jit(solution)/shard_map/ppermute | solution.py:30
  12.3 34.1 %collective-permute-start.3 = (bf16[256,1024]{1,0:T(8,128)(2,1)}, bf16[256,1024]{1,0:T(8,128)(2,1)}, u32[]{:S(2)}, u32[]{:S(2)}) collective-permute-start(bf16[256,1024]{1,0:T(8,128)(2,1)} %param.21), channel_id=1, source_target_pairs={{0,3},{1,0},{2,1},{3,2},{4,7},{5,4},{6,5},{7,6},{8,11},{9,8},{10,9... | collective-permute-start | bytes 1572872 | tf_op jit(solution)/shard_map/ppermute | solution.py:30
  12.4 43.9 %collective-permute-start.4 = (bf16[256,1024]{1,0:T(8,128)(2,1)}, bf16[256,1024]{1,0:T(8,128)(2,1)}, u32[]{:S(2)}, u32[]{:S(2)}) collective-permute-start(bf16[256,1024]{1,0:T(8,128)(2,1)} %param.21), channel_id=1, source_target_pairs={{0,2},{1,3},{2,0},{3,1},{4,6},{5,7},{6,4},{7,5},{8,10},{9,11},{10,... | collective-permute-start | bytes 1572872 | tf_op jit(solution)/shard_map/ppermute | solution.py:30
  14.1 42.2 %collective-permute-start.5 = (bf16[256,1024]{1,0:T(8,128)(2,1)}, bf16[256,1024]{1,0:T(8,128)(2,1)}, u32[]{:S(2)}, u32[]{:S(2)}) collective-permute-start(bf16[256,1024]{1,0:T(8,128)(2,1)} %param.21), channel_id=1, source_target_pairs={{0,1},{1,2},{2,3},{3,0},{4,5},{5,6},{6,7},{7,4},{8,9},{9,10},{10,1... | collective-permute-start | bytes 1572872 | tf_op jit(solution)/shard_map/ppermute | solution.py:30
  38.2 18.1 %copy-start.8 = (bf16[256,1024]{1,0:T(8,128)(2,1)S(1)}, bf16[256,1024]{1,0:T(8,128)(2,1)}, u32[]{:S(2)}) copy-start(bf16[256,1024]{1,0:T(8,128)(2,1)} %param.21) | copy-start | bytes 1572868
  46.4 41.4 %collective-permute-start.2 = (bf16[256,1024]{1,0:T(8,128)(2,1)S(1)}, bf16[256,1024]{1,0:T(8,128)(2,1)}, u32[]{:S(2)}, u32[]{:S(2)}) collective-permute-start(bf16[256,1024]{1,0:T(8,128)(2,1)S(1)} %bitcast.126), channel_id=1, source_target_pairs={{0,1},{1,2},{2,3},{3,0},{4,5},{5,6},{6,7},{7,4},{8,9},{9,10},{10,1... | collective-permute-start | bytes 1572872 | tf_op jit(solution)/shard_map/ppermute | solution.py:30
  83.9 2.0 copy-start.1
  87.6 68.7 %all-gather.8.cloned.1.call-start = ((), (), s32[]{:S(2)}) async-start(), calls=%async_computation.2 | async-start | bytes 1966080 | tf_op jit(solution)/shard_map/all_gather | solution.py:121
  87.8 4.8 %copy-start.2 = (f32[2,512,1024]{2,1,0:T(8,128)S(1)}, f32[2,512,1024]{2,1,0:T(8,128)}, u32[]{:S(2)}) copy-start(f32[2,512,1024]{2,1,0:T(8,128)} %copy-done.1) | copy-start | bytes 12582916
  93.5 24.9 %copy-start.10 = (f32[2,1024]{1,0:T(2,128)S(1)}, f32[2,1024]{1,0:T(2,128)}, u32[]{:S(2)}) copy-start(f32[2,1024]{1,0:T(2,128)} %param.22) | copy-start | bytes 24580
  116.7 16.7 %copy-start.6 = (bf16[512,1024]{1,0:T(8,128)(2,1)S(1)}, bf16[512,1024]{1,0:T(8,128)(2,1)}, u32[]{:S(2)}) copy-start(bf16[512,1024]{1,0:T(8,128)(2,1)} %param.19) | copy-start | bytes 3145732
  116.7 7.5 %collective-permute-start.6 = (bf16[256,512]{1,0:T(8,128)(2,1)S(1)}, bf16[256,512]{1,0:T(8,128)(2,1)S(1)}, u32[]{:S(2)}, u32[]{:S(2)}) collective-permute-start(bf16[256,512]{1,0:T(8,128)(2,1)S(1)} %bitcast.130), channel_id=1, source_target_pairs={{0,3},{1,0},{2,1},{3,2},{4,7},{5,4},{6,5},{7,6},{8,11},{9,8},{10,9... | collective-permute-start | bytes 786440 | tf_op jit(solution)/shard_map/ppermute | solution.py:30
  117.6 13.3 %collective-permute-start.7 = (bf16[256,512]{1,0:T(8,128)(2,1)S(1)}, bf16[256,512]{1,0:T(8,128)(2,1)S(1)}, u32[]{:S(2)}, u32[]{:S(2)}) collective-permute-start(bf16[256,512]{1,0:T(8,128)(2,1)S(1)} %bitcast.131), channel_id=1, source_target_pairs={{0,2},{1,3},{2,0},{3,1},{4,6},{5,7},{6,4},{7,5},{8,10},{9,11},{10,... | collective-permute-start | bytes 786440 | tf_op jit(solution)/shard_map/ppermute | solution.py:30
  118.3 12.8 %collective-permute-start.8 = (bf16[256,512]{1,0:T(8,128)(2,1)S(1)}, bf16[256,512]{1,0:T(8,128)(2,1)}, u32[]{:S(2)}, u32[]{:S(2)}) collective-permute-start(bf16[256,512]{1,0:T(8,128)(2,1)S(1)} %bitcast.132), channel_id=1, source_target_pairs={{0,1},{1,2},{2,3},{3,0},{4,5},{5,6},{6,7},{7,4},{8,9},{9,10},{10,1... | collective-permute-start | bytes 786440 | tf_op jit(solution)/shard_map/ppermute | solution.py:30
  118.5 89.1 %reduce-scatter.2.cloned.1.call-start = ((), (), s32[]{:S(2)}) async-start(), calls=%async_computation.3 | async-start | bytes 1966080 | tf_op jit(solution)/shard_map/reduce_scatter | solution.py:178
  118.6 14.8 %copy-start.3 = (bf16[4,256,1024]{2,1,0:T(8,128)(2,1)S(1)}, bf16[4,256,1024]{2,1,0:T(8,128)(2,1)}, u32[]{:S(2)}) copy-start(bf16[4,256,1024]{2,1,0:T(8,128)(2,1)} %fusion.14) | copy-start | bytes 6291460
  136.5 2.3 %copy-start.11 = (s32[1024]{0:T(1024)S(1)}, s32[1024]{0:T(1024)}, u32[]{:S(2)}) copy-start(s32[1024]{0:T(1024)} %param.17) | copy-start | bytes 12292
  136.5 2.3 %copy-start.13 = (f32[64]{0:T(128)S(1)}, f32[64]{0:T(128)}, u32[]{:S(2)}) copy-start(f32[64]{0:T(128)} %param.18) | copy-start | bytes 772
  137.1 15.5 %copy-start.5 = (bf16[4,256,1024]{2,1,0:T(8,128)(2,1)S(1)}, bf16[4,256,1024]{2,1,0:T(8,128)(2,1)}, u32[]{:S(2)}) copy-start(bf16[4,256,1024]{2,1,0:T(8,128)(2,1)} %fusion.21) | copy-start | bytes 6291460
  137.1 5.8 %collective-permute-start.9 = (bf16[256,512]{1,0:T(8,128)(2,1)S(1)}, bf16[256,512]{1,0:T(8,128)(2,1)S(1)}, u32[]{:S(2)}, u32[]{:S(2)}) collective-permute-start(bf16[256,512]{1,0:T(8,128)(2,1)S(1)} %bitcast.149), channel_id=1, source_target_pairs={{0,3},{1,0},{2,1},{3,2},{4,7},{5,4},{6,5},{7,6},{8,11},{9,8},{10,9... | collective-permute-start | bytes 786440 | tf_op jit(solution)/shard_map/ppermute | solution.py:30
  137.1 14.0 %collective-permute-start.10 = (bf16[256,512]{1,0:T(8,128)(2,1)S(1)}, bf16[256,512]{1,0:T(8,128)(2,1)S(1)}, u32[]{:S(2)}, u32[]{:S(2)}) collective-permute-start(bf16[256,512]{1,0:T(8,128)(2,1)S(1)} %bitcast.150), channel_id=1, source_target_pairs={{0,2},{1,3},{2,0},{3,1},{4,6},{5,7},{6,4},{7,5},{8,10},{9,11},{10,... | collective-permute-start | bytes 786440 | tf_op jit(solution)/shard_map/ppermute | solution.py:30
  138.6 12.7 %collective-permute-start.11 = (bf16[256,512]{1,0:T(8,128)(2,1)S(1)}, bf16[256,512]{1,0:T(8,128)(2,1)S(1)}, u32[]{:S(2)}, u32[]{:S(2)}) collective-permute-start(bf16[256,512]{1,0:T(8,128)(2,1)S(1)} %bitcast.151), channel_id=1, source_target_pairs={{0,1},{1,2},{2,3},{3,0},{4,5},{5,6},{6,7},{7,4},{8,9},{9,10},{10,1... | collective-permute-start | bytes 786440 | tf_op jit(solution)/shard_map/ppermute | solution.py:30
  152.6 2.8 %copy-start.7 = (bf16[2,1024,256]{2,1,0:T(8,128)(2,1)S(1)}, bf16[2,1024,256]{2,1,0:T(8,128)(2,1)}, u32[]{:S(2)}) copy-start(bf16[2,1024,256]{2,1,0:T(8,128)(2,1)} %param.25) | copy-start | bytes 3145732
  163.2 1.2 collective-permute-start.12
  164.4 3.6 %collective-permute-start.13 = (f32[1024]{0:T(1024)S(1)}, f32[1024]{0:T(1024)S(1)}, u32[]{:S(2)}, u32[]{:S(2)}) collective-permute-start(f32[1024]{0:T(1024)S(1)} %add.61), channel_id=1, source_target_pairs={{0,2},{1,3},{2,0},{3,1},{4,6},{5,7},{6,4},{7,5},{8,10},{9,11},{10,... | collective-permute-start | bytes 12296 | tf_op jit(solution)/shard_map/ppermute | solution.py:58
  165.3 4.6 %slice-start = ((s8[6291456]{0:T(1024)(128)(4,1)}), s8[4194304]{0:T(1024)(128)(4,1)S(1)}, s32[]{:S(2)}) async-start(s8[6291456]{0:T(1024)(128)(4,1)} %bitcast.120), calls=%async_computation.5 | async-start | bytes 8388608
  168.6 1.6 slice-start.1
  (2 other events, 2.2 us)
Sparse Core Ops, SparseCore 0:
  9.6 66.2 all-gather.5
  87.7 26.9 all-gather.9
  118.7 36.9 all-gather.7
  173.5 34.0 reduce-scatter.1
where the time goes:
time: 216 us
  waiting for transfers between devices  97 us (45%)
  other arithmetic  45.7 us (21%)
  matrix products  26.8 us (12%)
  between operations  14.2 us (7%)
  blocking collectives  13.3 us (6%)
  starting transfers between devices  10.7 us (5%)
  local copies, waits for them, and re-layouts  8.39 us (4%)
    ppermute x12, waiting for transfers between devices, ring_gather(): blocks.append(lax.ppermute(x, axis, [(i, (i - s) % n) for i in range(n)]))  38.8 us
    reduce_scatter x1, waiting for transfers between devices, on_device(): lax.psum_scatter(jnp.dot(enc.T, dquery, preferred_element_type=jnp.float3...  32.4 us
    another operation x1, other arithmetic  22.8 us
    all_gather x1, waiting for transfers between devices, on_device(): piece = lax.all_gather(kv_weight, 'picks', axis=0, tiled=True)  14.5 us
    concatenate x4, other arithmetic, ring_gather(): ordered = jnp.roll(flipped, idx, axis=0)  13.3 us
    all_gather x1, blocking collectives, on_device(): lax.all_gather(jnp.stack([top, total]), 'picks', axis=0, tiled=False)  13.3 us
    ppermute x12, starting transfers between devices, ring_gather(): blocks.append(lax.ppermute(x, axis, [(i, (i - s) % n) for i in range(n)]))  9.4 us
    all_gather x1, waiting for transfers between devices, on_device(): lax.all_gather(numer.astype(jnp.bfloat16), 'picks', axis=0, tiled=False)  7.77 us
  transfers between devices with their start and end apart: 18, of which 13 were waited for; matrix products, arithmetic and copies ran while one was open for 28% of the time, Pallas kernels for 0%

commit v1 on v0

--- a/solution.py
+++ b/solution.py
@@ -10,6 +10,12 @@
 PI = 3.141592653589793
 EPS = 1e-06
 RING_MAX = 4
+
+
+def in_order(parts, dim):
+    shape = list(parts.shape[1:])
+    shape[dim] *= parts.shape[0]
+    return jnp.moveaxis(parts, 0, dim).reshape(shape)
 
 
 def encode(coords):
@@ -86,7 +92,19 @@
     column = lax.axis_index("heads") * local
     enc = encode(coords)
     cross_full = ring_gather(cross_out, "heads", n_heads)
-    piece = lax.all_gather(kv_weight, "picks", axis=0, tiled=True)
+    size = lax.axis_size("picks")
+    pairs = [(i_2, (i_2 + 1) % size) for i_2 in range(size)]
+    back = [(b, a) for a, b in pairs]
+    lower, upper = ([], [])
+    for step in range(size - 1):
+        if step % 2 == 0:
+            lower.append(lax.ppermute(lower[-1] if lower else kv_weight, "picks", pairs))
+        else:
+            upper.append(lax.ppermute(upper[-1] if upper else kv_weight, "picks", back))
+    pieces = jnp.stack([*lower[::-1], kv_weight, *upper])
+    shift = lax.axis_index("picks") - len(lower)
+    pieces = pieces[(jnp.arange(size) - shift) % size]
+    piece = in_order(pieces, 0)
     cross_full, piece = lax.optimization_barrier((cross_full, piece))
     keys_vals = jnp.einsum("tf,fjc->tjc", enc, piece, preferred_element_type=jnp.float32).astype(
         jnp.bfloat16

time: 216 us -> 257 us (1.19)
  waiting for transfers between devices: 97 us -> 116 us
  local copies, waits for them, and re-layouts: 8.39 us -> 18.2 us
  other arithmetic: 45.7 us -> 52 us
  starting transfers between devices: 10.7 us -> 14.7 us
    ppermute x0 -> x3, waiting for transfers between devices: none -> 26.9 us  [the longest x2 17.3 us: on_device(): lax.ppermute(lower[-1] if lower else kv_weight, 'picks', pairs)]
    all_gather x1 -> x0, waiting for transfers between devices: 14.5 us -> none  [on_device(): piece = lax.all_gather(kv_weight, 'picks', axis=0, tiled=True)]
    gather x0 -> x1, local copies, waits for them, and re-layouts: none -> 9.81 us  [on_device(): pieces = pieces[(jnp.arange(size) - shift) % size]]
    another operation x1 -> x2, other arithmetic: 22.8 us -> 29.4 us
    ppermute x0 -> x3, starting transfers between devices: none -> 5.12 us  [the longest x1 3.54 us: on_device(): upper.append(lax.ppermute(upper[-1] if upper else kv_weight, 'picks', back))]
    ppermute x12, waiting for transfers between devices: 38.8 us -> 42.8 us  [ring_gather(): blocks.append(lax.ppermute(x, axis, [(i, (i - s) % n) for i in range(n)]))]
    all_gather x1, waiting for transfers between devices: 7.77 us -> 11.1 us  [on_device(): lax.all_gather(numer.astype(jnp.bfloat16), 'picks', axis=0, tiled=False)]
    concatenate x4 -> x3, other arithmetic: 13.3 us -> 10.8 us  [ring_gather(): ordered = jnp.roll(flipped, idx, axis=0)]
  transfers between devices with their start and end apart: 18 -> 20, of which waited for: 13 -> 14; matrix products, arithmetic and copies ran while one was open for 28% -> 20% of each run, Pallas kernels for 0% -> 0%
where the time goes in v1:
time: 257 us
  waiting for transfers between devices  116 us (45%)
  other arithmetic  52 us (20%)
  matrix products  28 us (11%)
  local copies, waits for them, and re-layouts  18.2 us (7%)
  starting transfers between devices  14.7 us (6%)
  between operations  14.2 us (6%)
  blocking collectives  13.5 us (5%)
    ppermute x12, waiting for transfers between devices, ring_gather(): blocks.append(lax.ppermute(x, axis, [(i, (i - s) % n) for i in range(n)]))  42.8 us
    reduce_scatter x1, waiting for transfers between devices, on_device(): lax.psum_scatter(jnp.dot(enc.T, dquery, preferred_element_type=jnp.float3...  32.4 us
    another operation x1, other arithmetic  22.8 us
    ppermute x2, waiting for transfers between devices, on_device(): lax.ppermute(lower[-1] if lower else kv_weight, 'picks', pairs)  17.3 us
    all_gather x1, blocking collectives, on_device(): lax.all_gather(jnp.stack([top, total]), 'picks', axis=0, tiled=False)  13.5 us
    all_gather x1, waiting for transfers between devices, on_device(): lax.all_gather(numer.astype(jnp.bfloat16), 'picks', axis=0, tiled=False)  11.1 us
    concatenate x3, other arithmetic, ring_gather(): ordered = jnp.roll(flipped, idx, axis=0)  10.8 us
    gather x1, local copies, waits for them, and re-layouts, on_device(): pieces = pieces[(jnp.arange(size) - shift) % size]  9.81 us
  transfers between devices with their start and end apart: 20, of which 14 were waited for; matrix products, arithmetic and copies ran while one was open for 20% of the time, Pallas kernels for 0%

profile of v1, /device:TPU:0, one launch (start us, length us, event | category | flops | bytes accessed | tf_op | source)
XLA Modules:
  0.0 256.8 jit_solution(577362407669138862)
XLA Ops:
  7.2 2.4 collective-permute-start.3
  13.1 1.6 collective-permute-start.6
  15.9 6.2 %collective-permute-done.3 = bf16[256,1024]{1,0:T(8,128)(2,1)} collective-permute-done((bf16[256,1024]{1,0:T(8,128)(2,1)}, bf16[256,1024]{1,0:T(8,128)(2,1)}, u32[]{:S(2)}, u32[]{:S(2)}) %collective-permute-start.3) | collective-permute-done | bytes 524320 | tf_op jit(solution)/shard_map/ppermute | solution.py:36
  22.9 11.7 %collective-permute-done.4 = bf16[256,1024]{1,0:T(8,128)(2,1)} collective-permute-done((bf16[256,1024]{1,0:T(8,128)(2,1)}, bf16[256,1024]{1,0:T(8,128)(2,1)}, u32[]{:S(2)}, u32[]{:S(2)}) %collective-permute-start.4) | collective-permute-done | bytes 524320 | tf_op jit(solution)/shard_map/ppermute | solution.py:36
  34.6 22.8 %fusion = (bf16[3,512,1024]{2,1,0:T(8,128)(2,1)S(1)}, bf16[3,512,1024]{2,1,0:T(8,128)(2,1)S(1)}) fusion(f32[3,1024]{1,0:T(4,128)S(1)} %copy-done.9, f32[512]{0:T(512)S(1)} %maximum_multiply_fusion), kind=kLoop, calls=%fused_computation.3 | loop fusion | flops 4718592 | bytes 6305792 | tf_op jit(solution)/shard_map/convert
  57.4 3.2 %pad_maximum_fusion = bf16[6,512,1024]{2,1,0:T(8,128)(2,1)} fusion(bf16[3,512,1024]{2,1,0:T(8,128)(2,1)S(1)} %get-tuple-element.29, bf16[3,512,1024]{2,1,0:T(8,128)(2,1)S(1)} %get-tuple-element.28), kind=kLoop, calls=%fused_computation.5 | loop fusion | flops 3145728 | bytes 12582912 | tf_op jit(solution)/shard_map/concatenate | solution.py:24
  60.6 3.5 %collective-permute-start.8 = (bf16[768,2,256]{2,1,0:T(2,128)(2,1)S(1)}, bf16[768,2,256]{2,1,0:T(2,128)(2,1)S(1)}, u32[]{:S(2)}, u32[]{:S(2)}) collective-permute-start(bf16[768,2,256]{2,1,0:T(2,128)(2,1)S(1)} %copy-done.7), channel_id=1, source_target_pairs={{4,0},{8,4},{12,8},{0,12},{5,1},{9,5},{13,9},{1,13},{6,2},{10,6},{... | collective-permute-start | bytes 2359304 | tf_op jit(solution)/shard_map/ppermute | solution.py:103
  64.2 8.3 %fusion.14 = (bf16[4,256,1024]{2,1,0:T(8,128)(2,1)}, bf16[4,256,1024]{2,1,0:T(8,128)(2,1)}) fusion(s32[]{:T(128)S(6)} %select_n.52, bf16[1,256,1024]{2,1,0:T(8,128)(2,1)S(1)} %bitcast.155, bf16[1,256,1024]{2,1,0:T(8,128)(2,1)} %bitcast.13, bf16[1,256,1024]{2,1,0:T(8,128)(2,1)} %bitcast.14, bf16[1,256,1024]{2,1,0:T(8,128)(2,1)} %bitcast.15, ...), kind=kLoop, calls=%fused_computation.40 | loop fusion | flops 14680064 | bytes 8388612 | tf_op jit(solution)/shard_map/jit(_roll_dynamic)/concatenate | solution.py:38
  72.5 9.5 %collective-permute-done.8 = bf16[768,2,256]{2,1,0:T(2,128)(2,1)S(1)} collective-permute-done((bf16[768,2,256]{2,1,0:T(2,128)(2,1)S(1)}, bf16[768,2,256]{2,1,0:T(2,128)(2,1)S(1)}, u32[]{:S(2)}, u32[]{:S(2)}) %collective-permute-start.8) | collective-permute-done | bytes 786464 | tf_op jit(solution)/shard_map/ppermute | solution.py:103
  82.1 17.3 %collective-permute-done.7 = bf16[768,2,256]{2,1,0:T(2,128)(2,1)S(1)} collective-permute-done((bf16[768,2,256]{2,1,0:T(2,128)(2,1)S(1)}, bf16[768,2,256]{2,1,0:T(2,128)(2,1)S(1)}, u32[]{:S(2)}, u32[]{:S(2)}) %collective-permute-start.7) | collective-permute-done | bytes 786464 | tf_op jit(solution)/shard_map/ppermute | solution.py:101
  99.4 6.6 %pad_maximum_fusion.1 = bf16[4,768,2,256]{3,2,1,0:T(2,128)(2,1)} fusion(bf16[1,768,2,256]{3,2,1,0:T(2,128)(2,1)S(1)} %bitcast.153, bf16[1,768,2,256]{3,2,1,0:T(2,128)(2,1)S(1)} %bitcast.151, bf16[1,768,2,256]{3,2,1,0:T(2,128)(2,1)S(1)} %bitcast.152, bf16[1,768,2,256]{3,2,1,0:T(2,128)(2,1)S(1)} %bitcast.154), kind=kLoop, calls=%fused_computation.32 | loop fusion | flops 4718592 | bytes 6291456 | tf_op jit(solution)/shard_map/stack | solution.py:104
  106.0 9.8 %gather_fusion = bf16[4,768,2,256]{3,2,1,0:T(2,128)(2,1)} fusion(bf16[4,768,2,256]{3,2,1,0:T(2,128)(2,1)} %pad_maximum_fusion.1, s32[1024]{0:T(1024)S(1)} %pad_clamp_fusion), kind=kCustom, calls=%fused_computation | custom fusion | bytes 6291472 | tf_op jit(solution)/shard_map/gather | solution.py:106
  115.8 7.1 %fusion.32 = bf16[1024,2,256]{0,2,1:T(8,128)(2,1)S(1)} fusion(bf16[3072,1024,1]{1,0,2:T(8,128)(2,1)} %bitcast.125, bf16[3072,2,256]{2,1,0:T(2,128)(2,1)} %bitcast.131), kind=kOutput, calls=%fused_computation.83 | convolution fusion | flops 3221749760 | bytes 10485760 | tf_op jit(solution)/shard_map/tf,fjc->tjc/dot_general | solution.py:109
  123.9 2.1 copy-done.2
  126.0 1.6 fusion.43
  127.6 3.1 %fusion.4 = f32[2,512]{1,0:T(2,128)S(1)} fusion(f32[2,512,1024]{2,1,0:T(8,128)} %copy-done.2, f32[2,512]{1,0:T(2,128)S(1)} %get-tuple-element.32), kind=kLoop, calls=%fused_computation.30 | loop fusion | flops 3144704 | bytes 4202496 | tf_op jit(solution)/shard_map/reduce_sum | solution.py:118
  130.7 13.5 %all-gather.1 = f32[8,2,512]{2,1,0:T(2,128)S(1)} all-gather(f32[2,2,512]{2,1,0:T(2,128)S(1)} %pad_maximum_fusion.2), channel_id=3, replica_groups=mesh['groups'=2,'picks'=4,'heads'=4] {'picks'}, dimensions={0}, use_global_device_ids=true | all-gather | bytes 40960 | tf_op jit(solution)/shard_map/all_gather | solution.py:123
  144.2 11.1 %all-gather.7.cloned.1.call-done = bf16[8,512,128]{2,1,0:T(8,128)(2,1)} async-done(((bf16[2,512,128]{2,1,0:T(8,128)(2,1)}), bf16[8,512,128]{2,1,0:T(8,128)(2,1)}) %all-gather.7.cloned.1.call-update) | async-done | bytes 1048592 | tf_op jit(solution)/shard_map/all_gather | solution.py:122
  155.3 1.8 multiply_reduce_fusion.2
  159.2 5.4 %collective-permute-done.9 = bf16[256,512]{1,0:T(8,128)(2,1)S(1)} collective-permute-done((bf16[256,512]{1,0:T(8,128)(2,1)S(1)}, bf16[256,512]{1,0:T(8,128)(2,1)S(1)}, u32[]{:S(2)}, u32[]{:S(2)}) %collective-permute-start.9) | collective-permute-done | bytes 262176 | tf_op jit(solution)/shard_map/ppermute | solution.py:36
  164.6 6.9 %collective-permute-done.10 = bf16[256,512]{1,0:T(8,128)(2,1)S(1)} collective-permute-done((bf16[256,512]{1,0:T(8,128)(2,1)S(1)}, bf16[256,512]{1,0:T(8,128)(2,1)S(1)}, u32[]{:S(2)}, u32[]{:S(2)}) %collective-permute-start.10) | collective-permute-done | bytes 262176 | tf_op jit(solution)/shard_map/ppermute | solution.py:36
  172.9 2.6 %multiply_reduce_fusion.4 = (f32[512]{0:T(512)S(1)}, f32[512,1024]{1,0:T(8,128)S(1)}) fusion(bf16[1024,512]{1,0:T(8,128)(2,1)S(1)} %bitcast.130, bf16[1024,1024]{1,0:T(8,128)(2,1)S(1)} %bitcast.124, bf16[512,1024]{1,0:T(8,128)(2,1)} %param.19), kind=kOutput, calls=%fused_computation.77 | convolution fusion | flops 1075838464 | bytes 6293504 | tf_op jit(solution)/shard_map/dot_general | solution.py:141
  177.9 1.4 collective-permute-start.13
  179.6 4.2 %collective-permute-done.12 = bf16[256,512]{1,0:T(8,128)(2,1)S(1)} collective-permute-done((bf16[256,512]{1,0:T(8,128)(2,1)S(1)}, bf16[256,512]{1,0:T(8,128)(2,1)S(1)}, u32[]{:S(2)}, u32[]{:S(2)}) %collective-permute-start.12) | collective-permute-done | bytes 262176 | tf_op jit(solution)/shard_map/ppermute | solution.py:36
  183.7 8.0 %collective-permute-done.13 = bf16[256,512]{1,0:T(8,128)(2,1)S(1)} collective-permute-done((bf16[256,512]{1,0:T(8,128)(2,1)S(1)}, bf16[256,512]{1,0:T(8,128)(2,1)S(1)}, u32[]{:S(2)}, u32[]{:S(2)}) %collective-permute-start.13) | collective-permute-done | bytes 262176 | tf_op jit(solution)/shard_map/ppermute | solution.py:36
  193.2 1.4 multiply_reduce_fusion.3
  196.9 5.1 %convolution_convert_fusion.2 = bf16[1024,256]{0,1:T(8,128)(2,1)S(1)} fusion(bf16[3072,1024]{1,0:T(8,128)(2,1)} %bitcast.126, bf16[3072,256]{1,0:T(8,128)(2,1)} %all-gather.5.cloned.1.call-done), kind=kOutput, calls=%fused_computation.86 | convolution fusion | flops 1610874880 | bytes 8388608 | tf_op jit(solution)/shard_map/dot_general | solution.py:171
  206.6 2.0 collective-permute-done.16
  210.9 3.1 %convolution_convert_fusion = bf16[3072,256]{1,0:T(8,128)(2,1)} fusion(bf16[3072,1024]{1,0:T(8,128)(2,1)S(1)} %bitcast.129, bf16[1024,256]{0,1:T(8,128)(2,1)S(1)} %bitcast.180), kind=kOutput, calls=%fused_computation.27 | convolution fusion | flops 1611399168 | bytes 8388608 | tf_op jit(solution)/shard_map/dot_general | solution.py:197
  214.0 1.9 constant_dynamic-slice_fusion
  215.9 32.4 %reduce-scatter.2.cloned.1.call-done = bf16[768,256]{1,0:T(8,128)(2,1)} async-done(((bf16[3072,256]{1,0:T(8,128)(2,1)}), bf16[768,256]{1,0:T(8,128)(2,1)}) %reduce-scatter.2.cloned.1.call-update) | async-done | bytes 393232 | tf_op jit(solution)/shard_map/reduce_scatter | solution.py:196
  248.3 1.9 convert_element_type.100
  (94 shorter events, 23.0 us)
Async XLA Ops:
  7.2 168.3 %copy-start = (bf16[3,1024,256]{2,1,0:T(8,128)(2,1)S(1)}, bf16[3,1024,256]{2,1,0:T(8,128)(2,1)}, u32[]{:S(2)}) copy-start(bf16[3,1024,256]{2,1,0:T(8,128)(2,1)} %param.23) | copy-start | bytes 4718596
  7.2 27.4 %copy-start.9 = (f32[3,1024]{1,0:T(4,128)S(1)}, f32[3,1024]{1,0:T(4,128)}, u32[]{:S(2)}) copy-start(f32[3,1024]{1,0:T(4,128)} %param.16) | copy-start | bytes 36868
  7.2 148.1 %all-gather.7.cloned.1.call-start = ((), (), s32[]{:S(2)}) async-start(), calls=%async_computation.3 | async-start | bytes 1310720 | tf_op jit(solution)/shard_map/all_gather | solution.py:122
  7.2 14.9 %collective-permute-start.3 = (bf16[256,1024]{1,0:T(8,128)(2,1)}, bf16[256,1024]{1,0:T(8,128)(2,1)}, u32[]{:S(2)}, u32[]{:S(2)}) collective-permute-start(bf16[256,1024]{1,0:T(8,128)(2,1)} %param.21), channel_id=1, source_target_pairs={{0,3},{1,0},{2,1},{3,2},{4,7},{5,4},{6,5},{7,6},{8,11},{9,8},{10,9... | collective-permute-start | bytes 1572872 | tf_op jit(solution)/shard_map/ppermute | solution.py:36
  9.7 24.9 %collective-permute-start.4 = (bf16[256,1024]{1,0:T(8,128)(2,1)}, bf16[256,1024]{1,0:T(8,128)(2,1)}, u32[]{:S(2)}, u32[]{:S(2)}) collective-permute-start(bf16[256,1024]{1,0:T(8,128)(2,1)} %param.21), channel_id=1, source_target_pairs={{0,2},{1,3},{2,0},{3,1},{4,6},{5,7},{6,4},{7,5},{8,10},{9,11},{10,... | collective-permute-start | bytes 1572872 | tf_op jit(solution)/shard_map/ppermute | solution.py:36
  10.3 50.3 %collective-permute-start.5 = (bf16[256,1024]{1,0:T(8,128)(2,1)}, bf16[256,1024]{1,0:T(8,128)(2,1)}, u32[]{:S(2)}, u32[]{:S(2)}) collective-permute-start(bf16[256,1024]{1,0:T(8,128)(2,1)} %param.21), channel_id=1, source_target_pairs={{0,1},{1,2},{2,3},{3,0},{4,5},{5,6},{6,7},{7,4},{8,9},{9,10},{10,1... | collective-permute-start | bytes 1572872 | tf_op jit(solution)/shard_map/ppermute | solution.py:36
  11.7 52.5 %collective-permute-start.2 = (bf16[256,1024]{1,0:T(8,128)(2,1)S(1)}, bf16[256,1024]{1,0:T(8,128)(2,1)}, u32[]{:S(2)}, u32[]{:S(2)}) collective-permute-start(bf16[256,1024]{1,0:T(8,128)(2,1)S(1)} %bitcast.132), channel_id=1, source_target_pairs={{0,1},{1,2},{2,3},{3,0},{4,5},{5,6},{6,7},{7,4},{8,9},{9,10},{10,1... | collective-permute-start | bytes 1572872 | tf_op jit(solution)/shard_map/ppermute | solution.py:36
  13.1 51.1 %collective-permute-start.6 = (bf16[768,2,256]{2,1,0:T(2,128)(2,1)}, bf16[768,2,256]{2,1,0:T(2,128)(2,1)S(1)}, u32[]{:S(2)}, u32[]{:S(2)}) collective-permute-start(bf16[768,2,256]{2,1,0:T(2,128)(2,1)} %param.20), channel_id=1, source_target_pairs={{0,4},{4,8},{8,12},{12,0},{1,5},{5,9},{9,13},{13,1},{2,6},{6,10},{... | collective-permute-start | bytes 2359304 | tf_op jit(solution)/shard_map/ppermute | solution.py:101
  22.2 42.0 %collective-permute-start.1 = (bf16[256,1024]{1,0:T(8,128)(2,1)S(1)}, bf16[256,1024]{1,0:T(8,128)(2,1)}, u32[]{:S(2)}, u32[]{:S(2)}) collective-permute-start(bf16[256,1024]{1,0:T(8,128)(2,1)S(1)} %bitcast.133), channel_id=1, source_target_pairs={{0,2},{1,3},{2,0},{3,1},{4,6},{5,7},{6,4},{7,5},{8,10},{9,11},{10,... | collective-permute-start | bytes 1572872 | tf_op jit(solution)/shard_map/ppermute | solution.py:36
  34.6 29.6 %collective-permute-start = (bf16[256,1024]{1,0:T(8,128)(2,1)S(1)}, bf16[256,1024]{1,0:T(8,128)(2,1)}, u32[]{:S(2)}, u32[]{:S(2)}) collective-permute-start(bf16[256,1024]{1,0:T(8,128)(2,1)S(1)} %bitcast.134), channel_id=1, source_target_pairs={{0,3},{1,0},{2,1},{3,2},{4,7},{5,4},{6,5},{7,6},{8,11},{9,8},{10,9... | collective-permute-start | bytes 1572872 | tf_op jit(solution)/shard_map/ppermute | solution.py:36
  57.4 3.2 %copy-start.7 = (bf16[768,2,256]{2,1,0:T(2,128)(2,1)S(1)}, bf16[768,2,256]{2,1,0:T(2,128)(2,1)}, u32[]{:S(2)}) copy-start(bf16[768,2,256]{2,1,0:T(2,128)(2,1)} %param.20) | copy-start | bytes 2359300
  57.4 6.8 %copy-start.8 = (bf16[256,1024]{1,0:T(8,128)(2,1)S(1)}, bf16[256,1024]{1,0:T(8,128)(2,1)}, u32[]{:S(2)}) copy-start(bf16[256,1024]{1,0:T(8,128)(2,1)} %param.21) | copy-start | bytes 1572868
  60.6 21.4 %collective-permute-start.8 = (bf16[768,2,256]{2,1,0:T(2,128)(2,1)S(1)}, bf16[768,2,256]{2,1,0:T(2,128)(2,1)S(1)}, u32[]{:S(2)}, u32[]{:S(2)}) collective-permute-start(bf16[768,2,256]{2,1,0:T(2,128)(2,1)S(1)} %copy-done.7), channel_id=1, source_target_pairs={{4,0},{8,4},{12,8},{0,12},{5,1},{9,5},{13,9},{1,13},{6,2},{10,6},{... | collective-permute-start | bytes 2359304 | tf_op jit(solution)/shard_map/ppermute | solution.py:103
  64.2 35.2 %collective-permute-start.7 = (bf16[768,2,256]{2,1,0:T(2,128)(2,1)S(1)}, bf16[768,2,256]{2,1,0:T(2,128)(2,1)S(1)}, u32[]{:S(2)}, u32[]{:S(2)}) collective-permute-start(bf16[768,2,256]{2,1,0:T(2,128)(2,1)S(1)} %collective-permute-done.6), channel_id=1, source_target_pairs={{0,4},{4,8},{8,12},{12,0},{1,5},{5,9},{9,13},{13,1},{2,6},{6,10},{... | collective-permute-start | bytes 2359304 | tf_op jit(solution)/shard_map/ppermute | solution.py:101
  127.6 69.3 %all-gather.5.cloned.1.call-start = ((), (), s32[]{:S(2)}) async-start(), calls=%async_computation.1 | async-start | bytes 1966080 | tf_op jit(solution)/shard_map/all_gather | solution.py:139
  130.7 28.4 %copy-start.10 = (f32[2,1024]{1,0:T(2,128)S(1)}, f32[2,1024]{1,0:T(2,128)}, u32[]{:S(2)}) copy-start(f32[2,1024]{1,0:T(2,128)} %param.22) | copy-start | bytes 24580
  157.4 7.3 %collective-permute-start.9 = (bf16[256,512]{1,0:T(8,128)(2,1)S(1)}, bf16[256,512]{1,0:T(8,128)(2,1)S(1)}, u32[]{:S(2)}, u32[]{:S(2)}) collective-permute-start(bf16[256,512]{1,0:T(8,128)(2,1)S(1)} %bitcast.138), channel_id=1, source_target_pairs={{0,3},{1,0},{2,1},{3,2},{4,7},{5,4},{6,5},{7,6},{8,11},{9,8},{10,9... | collective-permute-start | bytes 786440 | tf_op jit(solution)/shard_map/ppermute | solution.py:36
  158.2 13.4 %collective-permute-start.10 = (bf16[256,512]{1,0:T(8,128)(2,1)S(1)}, bf16[256,512]{1,0:T(8,128)(2,1)S(1)}, u32[]{:S(2)}, u32[]{:S(2)}) collective-permute-start(bf16[256,512]{1,0:T(8,128)(2,1)S(1)} %bitcast.139), channel_id=1, source_target_pairs={{0,2},{1,3},{2,0},{3,1},{4,6},{5,7},{6,4},{7,5},{8,10},{9,11},{10,... | collective-permute-start | bytes 786440 | tf_op jit(solution)/shard_map/ppermute | solution.py:36
  159.0 12.7 %collective-permute-start.11 = (bf16[256,512]{1,0:T(8,128)(2,1)S(1)}, bf16[256,512]{1,0:T(8,128)(2,1)S(1)}, u32[]{:S(2)}, u32[]{:S(2)}) collective-permute-start(bf16[256,512]{1,0:T(8,128)(2,1)S(1)} %bitcast.140), channel_id=1, source_target_pairs={{0,1},{1,2},{2,3},{3,0},{4,5},{5,6},{6,7},{7,4},{8,9},{9,10},{10,1... | collective-permute-start | bytes 786440 | tf_op jit(solution)/shard_map/ppermute | solution.py:36
  159.2 89.2 %reduce-scatter.2.cloned.1.call-start = ((), (), s32[]{:S(2)}) async-start(), calls=%async_computation.2 | async-start | bytes 1966080 | tf_op jit(solution)/shard_map/reduce_scatter | solution.py:196
  159.2 13.7 %copy-start.3 = (bf16[4,256,1024]{2,1,0:T(8,128)(2,1)S(1)}, bf16[4,256,1024]{2,1,0:T(8,128)(2,1)}, u32[]{:S(2)}) copy-start(bf16[4,256,1024]{2,1,0:T(8,128)(2,1)} %get-tuple-element.42) | copy-start | bytes 6291460
  177.2 2.2 copy-start.11
  177.3 2.2 copy-start.13
  177.8 15.4 %copy-start.5 = (bf16[4,256,1024]{2,1,0:T(8,128)(2,1)S(1)}, bf16[4,256,1024]{2,1,0:T(8,128)(2,1)}, u32[]{:S(2)}) copy-start(bf16[4,256,1024]{2,1,0:T(8,128)(2,1)} %get-tuple-element.43) | copy-start | bytes 6291460
  177.8 5.9 %collective-permute-start.12 = (bf16[256,512]{1,0:T(8,128)(2,1)S(1)}, bf16[256,512]{1,0:T(8,128)(2,1)S(1)}, u32[]{:S(2)}, u32[]{:S(2)}) collective-permute-start(bf16[256,512]{1,0:T(8,128)(2,1)S(1)} %bitcast.160), channel_id=1, source_target_pairs={{0,3},{1,0},{2,1},{3,2},{4,7},{5,4},{6,5},{7,6},{8,11},{9,8},{10,9... | collective-permute-start | bytes 786440 | tf_op jit(solution)/shard_map/ppermute | solution.py:36
  177.9 13.8 %collective-permute-start.13 = (bf16[256,512]{1,0:T(8,128)(2,1)S(1)}, bf16[256,512]{1,0:T(8,128)(2,1)S(1)}, u32[]{:S(2)}, u32[]{:S(2)}) collective-permute-start(bf16[256,512]{1,0:T(8,128)(2,1)S(1)} %bitcast.161), channel_id=1, source_target_pairs={{0,2},{1,3},{2,0},{3,1},{4,6},{5,7},{6,4},{7,5},{8,10},{9,11},{10,... | collective-permute-start | bytes 786440 | tf_op jit(solution)/shard_map/ppermute | solution.py:36
  179.3 12.7 %collective-permute-start.14 = (bf16[256,512]{1,0:T(8,128)(2,1)S(1)}, bf16[256,512]{1,0:T(8,128)(2,1)S(1)}, u32[]{:S(2)}, u32[]{:S(2)}) collective-permute-start(bf16[256,512]{1,0:T(8,128)(2,1)S(1)} %bitcast.162), channel_id=1, source_target_pairs={{0,1},{1,2},{2,3},{3,0},{4,5},{5,6},{6,7},{7,4},{8,9},{9,10},{10,1... | collective-permute-start | bytes 786440 | tf_op jit(solution)/shard_map/ppermute | solution.py:36
  193.2 2.8 %copy-start.6 = (bf16[2,1024,256]{2,1,0:T(8,128)(2,1)S(1)}, bf16[2,1024,256]{2,1,0:T(8,128)(2,1)}, u32[]{:S(2)}) copy-start(bf16[2,1024,256]{2,1,0:T(8,128)(2,1)} %param.25) | copy-start | bytes 3145732
  203.8 1.2 collective-permute-start.15
  205.1 3.6 %collective-permute-start.16 = (f32[1024]{0:T(1024)S(1)}, f32[1024]{0:T(1024)S(1)}, u32[]{:S(2)}, u32[]{:S(2)}) collective-permute-start(f32[1024]{0:T(1024)S(1)} %add.87), channel_id=1, source_target_pairs={{0,2},{1,3},{2,0},{3,1},{4,6},{5,7},{6,4},{7,5},{8,10},{9,11},{10,... | collective-permute-start | bytes 12296 | tf_op jit(solution)/shard_map/ppermute | solution.py:64
  205.8 4.7 %slice-start = ((s8[6291456]{0:T(1024)(128)(4,1)}), s8[4194304]{0:T(1024)(128)(4,1)S(1)}, s32[]{:S(2)}) async-start(s8[6291456]{0:T(1024)(128)(4,1)} %bitcast.127), calls=%async_computation.4 | async-start | bytes 8388608
  210.9 39.4 %copy-start.1 = (bf16[3,1024,256]{2,1,0:T(8,128)(2,1)S(1)}, bf16[3,1024,256]{2,1,0:T(8,128)(2,1)}, u32[]{:S(2)}) copy-start(bf16[3,1024,256]{2,1,0:T(8,128)(2,1)} %param.23) | copy-start | bytes 4718596
  (4 other events, 5.9 us)
Sparse Core Ops, SparseCore 0:
  127.7 27.5 all-gather.6
  159.3 36.8 all-gather.4
  214.1 34.1 reduce-scatter.1
